TPU v7x, 128 devices: a whole 4x4x4 slice. The times are simulated.
128 devices in a mesh: tm: 32 (over x, z, core), chan: 4 (over y).
Axes of the slice: x: 4, y: 4, z: 4, core: 2. Of those that a mesh axis runs over, the one named last changes fastest.
Arguments:
- inputs: bfloat16 [64, 256, 512], P('tm'), may hold values from -6 to 6
- decay: float32 [64, 512], P('tm', 'chan'), may hold values from 0 to 1, as said below
- kernel_b: bfloat16 [9, 512, 256], P(None, 'chan'), may hold values from -0.125 to 0.125
- kernel_c: bfloat16 [9, 256, 512], P(None, 'chan'), may hold values from -0.09375 to 0.09375
- cotangent: bfloat16 [64, 256, 512], P('tm', 'chan'), may hold values from -0.03125 to 0.03125
Outputs:
- grad_b: float32 [9, 512, 256], P(None, 'chan')
- grad_c: float32 [9, 256, 512], P(None, 'chan')
- decay_grad: float32 [64, 512], P('tm', 'chan')
Inputs may be any that keep to these rules, and one draw needn't show every extreme that they name: decay lies strictly between 0 and 1.
All inputs are finite; a program needn't handle non-finite values.
Results may differ from a plain program's by a relative error of at most 0.003.
Values may be sent and summed in bfloat16 or wider, within the bound.
No kernel may reach another device: no remote copies, remote signals or barrier semaphores. Data moves between devices by JAX's collectives and lax.ppermute only.
A program may use at most 128 MiB of HBM per device.

v0:
```python
import jax
import jax.numpy as jnp
from jax import lax
from jax.sharding import PartitionSpec as P

W = 64
offsets = ((-1, -1), (-1, 0), (-1, 1), (0, -1), (0, 0), (0, 1), (1, -1), (1, 0), (1, 1))


def passed_along(value, axis, steps):
    count = lax.axis_size(axis)
    first, last = (max(0, -steps), min(count, count - steps))
    return lax.ppermute(value, axis, [(source, source + steps) for source in range(first, last)])


def shift_cells(source, row_shift, col_shift, grid_width):
    cell_count = source.shape[-1]
    margin = grid_width + 1
    padded = jnp.pad(source, [(0, 0)] * (source.ndim - 1) + [(margin, margin)])
    first_cell = margin + row_shift * grid_width + col_shift
    shifted = lax.slice_in_dim(padded, first_cell, first_cell + cell_count, axis=source.ndim - 1)
    column = jnp.arange(cell_count) % grid_width
    inside = (column + col_shift >= 0) & (column + col_shift < grid_width)
    return jnp.where(inside, shifted, jnp.zeros((), source.dtype))


def stencil_stack(source, grid_width, decay_factor):
    parts = [
        shift_cells(source, decay_factor * pair[0], decay_factor * pair[1], grid_width)
        for pair in offsets
    ]
    return jnp.stack(parts, axis=source.ndim - 2)


def body(inputs, decay, kernel_b, kernel_c, cotangent):
    local_rows = kernel_b.shape[1]
    cell_count = inputs.shape[-1]
    blank_state = jnp.zeros((local_rows, cell_count), jnp.float32)
    input_stack = stencil_stack(inputs, W, 1)
    drives = jnp.einsum("kpc,fkcs->fps", kernel_b, input_stack, preferred_element_type=jnp.float32)

    def advance(current, frame_pair):
        frame_rate, drive = frame_pair
        current = frame_rate[:, None] * current + drive
        return (current, current)

    local_end, local_states = lax.scan(advance, blank_state, (decay, drives))
    decay_total = jnp.prod(decay, axis=0)

    def relay_state(turn_index, carried):
        outgoing = decay_total[:, None] * carried + local_end
        return passed_along(outgoing, "tm", 1)

    entering = lax.fori_loop(0, lax.axis_size("tm") - 1, relay_state, blank_state)
    cumulative = jnp.cumprod(decay, axis=0)
    states = local_states + cumulative[:, :, None] * entering[None]
    previous = jnp.concatenate([entering[None], states[:-1]], axis=0)
    states_bf = states.astype(jnp.bfloat16)
    cot_stack = stencil_stack(cotangent, W, -1)
    injected = lax.psum_scatter(
        jnp.einsum("kup,fkus->pfs", kernel_c, cot_stack, preferred_element_type=jnp.float32),
        "chan",
        scatter_dimension=0,
        tiled=True,
    )
    injected = jnp.moveaxis(injected, 1, 0)

    def retreat(carried, frame_pair):
        frame_rate, source = frame_pair
        adjoint = source + carried
        return (frame_rate[:, None] * adjoint, adjoint)

    message, local_adjoint = lax.scan(retreat, blank_state, (decay, injected), reverse=True)

    def relay_adjoint(turn_index, carried):
        outgoing = decay_total[:, None] * carried + message
        return passed_along(outgoing, "tm", -1)

    arriving = lax.fori_loop(0, lax.axis_size("tm") - 1, relay_adjoint, blank_state)
    suffix = jnp.flip(jnp.cumprod(jnp.flip(decay, 0), 0), 0)
    later_decay = jnp.concatenate([suffix[1:], jnp.ones_like(decay[:1])], axis=0)
    adjoint = local_adjoint + later_decay[:, :, None] * arriving[None]
    decay_grad = jnp.sum(adjoint * previous, axis=2)
    adjoint_bf = adjoint.astype(jnp.bfloat16)
    grad_b_part = jnp.einsum(
        "fps,fkcs->kpc", adjoint_bf, input_stack, preferred_element_type=jnp.float32
    )
    shifted = stencil_stack(lax.all_gather(states_bf, "chan", axis=1, tiled=True), W, 1)
    grad_c_part = jnp.einsum(
        "fus,fkps->kup", cotangent, shifted, preferred_element_type=jnp.float32
    )
    grad_b, grad_c = lax.psum((grad_b_part, grad_c_part), "tm")
    return (grad_b, grad_c, decay_grad)


def solution(mesh):
    in_specs = (
        P("tm", None, None),
        P("tm", "chan"),
        P(None, "chan", None),
        P(None, "chan", None),
        P("tm", "chan", None),
    )
    out_specs = (P(None, "chan", None), P(None, "chan", None), P("tm", "chan"))
    return jax.shard_map(body, mesh=mesh, in_specs=in_specs, out_specs=out_specs, check_vma=False)
```

profile of v0, /device:TPU:1, one launch (start us, length us, event | category | flops | bytes accessed | tf_op | source)
XLA Modules:
  0.0 817.5 jit_solution(8985757919530302460)
XLA Ops:
  20.7 275.2 %while.51 = (s32[]{:T(128)}, f32[128,512]{1,0:T(8,128)S(1)}, f32[128]{0:T(128)S(1)}, f32[128,512]{1,0:T(8,128)S(1)}, s32[]{:T(128)}) while((s32[]{:T(128)}, f32[128,512]{1,0:T(8,128)S(1)}, f32[128]{0:T(128)S(1)}, f32[128,512]{1,0:T(8,128)S(1)}, s32[]{:T(128)}) %tuple.101), condition=%wide.region_12.13_spmd, body=%wide.region_11.12_spmd.sunk | while | flops 131074 | bytes 1835621 | solution.py:54
  20.8 4.9 collective-permute-start.1
  29.1 4.4 collective-permute-start.1
  36.9 4.4 collective-permute-start.1
  44.7 4.4 collective-permute-start.1
  52.5 4.4 collective-permute-start.1
  60.2 4.4 collective-permute-start.1
  68.0 4.4 collective-permute-start.1
  75.8 4.4 collective-permute-start.1
  91.4 4.4 collective-permute-start.1
  99.2 4.4 collective-permute-start.1
  130.3 4.4 collective-permute-start.1
  138.1 6.0 collective-permute-start.1
  147.5 6.5 collective-permute-start.1
  157.4 6.5 collective-permute-start.1
  167.3 6.5 collective-permute-start.1
  177.2 6.5 collective-permute-start.1
  187.1 6.5 collective-permute-start.1
  197.0 6.5 collective-permute-start.1
  206.9 6.5 collective-permute-start.1
  216.8 6.5 collective-permute-start.1
  226.7 6.5 collective-permute-start.1
  236.6 6.5 collective-permute-start.1
  246.5 6.5 collective-permute-start.1
  256.4 6.5 collective-permute-start.1
  266.3 6.5 collective-permute-start.1
  276.2 6.5 collective-permute-start.1
  286.1 6.5 collective-permute-start.1
  300.5 49.7 %all-gather.2.cloned.1.call-done = bf16[2,512,512]{2,1,0:T(8,128)(2,1)} async-done(((bf16[2,128,512]{2,1,0:T(8,128)(2,1)}), bf16[2,512,512]{2,1,0:T(8,128)(2,1)}) %all-gather.2.cloned.1.call-update) | async-done | bytes 1048592 | tf_op jit(solution)/shard_map/all_gather | solution.py:88
  361.1 23.6 %reduce-scatter.2.cloned.1.call-done = f32[128,2,512]{0,2,1:T(8,128)} async-done(((f32[512,2,512]{0,2,1:T(8,128)}), f32[128,2,512]{0,2,1:T(8,128)}) %reduce-scatter.2.cloned.1.call-update) | async-done | bytes 524304 | tf_op jit(solution)/shard_map/reduce_scatter | solution.py:60
  387.4 279.4 %while.50 = (s32[]{:T(128)}, f32[128,512]{1,0:T(8,128)S(1)}, f32[128]{0:T(128)S(1)}, f32[128,512]{1,0:T(8,128)S(1)}, s32[]{:T(128)}) while((s32[]{:T(128)}, f32[128,512]{1,0:T(8,128)S(1)}, f32[128]{0:T(128)S(1)}, f32[128,512]{1,0:T(8,128)S(1)}, s32[]{:T(128)}) %tuple.113), condition=%wide.region_6.7_spmd, body=%wide.region_5.6_spmd.sunk | while | flops 131074 | bytes 1835621 | solution.py:79
  390.2 5.2 collective-permute-done
  397.4 5.8 collective-permute-done
  405.2 5.8 collective-permute-done
  413.0 5.8 collective-permute-done
  420.8 5.8 collective-permute-done
  428.5 5.8 collective-permute-done
  436.3 5.8 collective-permute-done
  444.1 5.8 collective-permute-done
  451.9 5.8 collective-permute-done
  459.7 5.8 collective-permute-done
  467.5 5.8 collective-permute-done
  475.3 5.8 collective-permute-done
  483.0 5.8 collective-permute-done
  490.8 7.7 collective-permute-done
  500.6 7.9 collective-permute-done
  510.5 7.9 collective-permute-done
  520.4 7.9 collective-permute-done
  530.3 7.9 collective-permute-done
  540.2 7.9 collective-permute-done
  550.0 7.9 collective-permute-done
  559.9 7.9 collective-permute-done
  569.8 7.9 collective-permute-done
  579.7 7.9 collective-permute-done
  589.6 7.9 collective-permute-done
  599.5 7.9 collective-permute-done
  609.4 7.9 collective-permute-done
  619.3 7.9 collective-permute-done
  629.2 7.9 collective-permute-done
  639.1 7.9 collective-permute-done
  649.0 7.9 collective-permute-done
  658.9 7.9 collective-permute-done
  666.8 4.8 convolution_bitcast_fusion.2
  672.4 133.6 %all-reduce.6.cloned.1.call-done = (f32[9,128,256]{1,2,0:T(8,128)}, f32[9,64,512]{2,1,0:T(8,128)}) async-done(((f32[9,128,256]{1,2,0:T(8,128)}, f32[9,64,512]{2,1,0:T(8,128)}), (f32[9,128,256]{1,2,0:T(8,128)}, f32[9,64,512]{2,1,0:T(8,128)})) %all-reduce.6.cloned.1.call-update) | async-done | bytes 2359312 | tf_op jit(solution)/shard_map/psum | solution.py:92
  (219 shorter events, 225.5 us)
Async XLA Ops:
  7.2 343.0 %all-gather.2.cloned.1.call-start = ((), (), s32[]{:S(2)}) async-start(), calls=%async_computation.2 | async-start | bytes 1310720 | tf_op jit(solution)/shard_map/all_gather | solution.py:88
  20.8 8.2 %collective-permute-start.1 = (f32[128,512]{1,0:T(8,128)S(1)}, f32[128,512]{1,0:T(8,128)S(1)}, u32[]{:S(2)}, u32[]{:S(2)}) collective-permute-start(f32[128,512]{1,0:T(8,128)S(1)} %multiply_add_fusion.8), channel_id=1, source_target_pairs={{0,4},{4,8},{8,12},{12,16},{16,20},{20,24},{24,28},{28,32},{32,36}... | collective-permute-start | bytes 786440 | tf_op jit(solution)/shard_map/while/body/eval_jaxpr/ppermute | solution.py:13
  29.1 7.7 collective-permute-start.1
  36.9 7.7 collective-permute-start.1
  44.7 7.7 collective-permute-start.1
  52.5 7.7 collective-permute-start.1
  60.2 7.7 collective-permute-start.1
  68.0 7.7 collective-permute-start.1
  75.8 7.7 collective-permute-start.1
  83.6 7.7 collective-permute-start.1
  91.4 7.7 collective-permute-start.1
  99.2 7.7 collective-permute-start.1
  107.0 7.7 collective-permute-start.1
  114.7 7.7 collective-permute-start.1
  122.5 7.7 collective-permute-start.1
  130.3 7.7 collective-permute-start.1
  138.1 9.3 %collective-permute-start.1 = (f32[128,512]{1,0:T(8,128)S(1)}, f32[128,512]{1,0:T(8,128)S(1)}, u32[]{:S(2)}, u32[]{:S(2)}) collective-permute-start(f32[128,512]{1,0:T(8,128)S(1)} %multiply_add_fusion.8), channel_id=1, source_target_pairs={{0,4},{4,8},{8,12},{12,16},{16,20},{20,24},{24,28},{28,32},{32,36}... | collective-permute-start | bytes 786440 | tf_op jit(solution)/shard_map/while/body/eval_jaxpr/ppermute | solution.py:13
  147.5 9.8 %collective-permute-start.1 = (f32[128,512]{1,0:T(8,128)S(1)}, f32[128,512]{1,0:T(8,128)S(1)}, u32[]{:S(2)}, u32[]{:S(2)}) collective-permute-start(f32[128,512]{1,0:T(8,128)S(1)} %multiply_add_fusion.8), channel_id=1, source_target_pairs={{0,4},{4,8},{8,12},{12,16},{16,20},{20,24},{24,28},{28,32},{32,36}... | collective-permute-start | bytes 786440 | tf_op jit(solution)/shard_map/while/body/eval_jaxpr/ppermute | solution.py:13
  157.4 9.8 %collective-permute-start.1 = (f32[128,512]{1,0:T(8,128)S(1)}, f32[128,512]{1,0:T(8,128)S(1)}, u32[]{:S(2)}, u32[]{:S(2)}) collective-permute-start(f32[128,512]{1,0:T(8,128)S(1)} %multiply_add_fusion.8), channel_id=1, source_target_pairs={{0,4},{4,8},{8,12},{12,16},{16,20},{20,24},{24,28},{28,32},{32,36}... | collective-permute-start | bytes 786440 | tf_op jit(solution)/shard_map/while/body/eval_jaxpr/ppermute | solution.py:13
  167.3 9.8 %collective-permute-start.1 = (f32[128,512]{1,0:T(8,128)S(1)}, f32[128,512]{1,0:T(8,128)S(1)}, u32[]{:S(2)}, u32[]{:S(2)}) collective-permute-start(f32[128,512]{1,0:T(8,128)S(1)} %multiply_add_fusion.8), channel_id=1, source_target_pairs={{0,4},{4,8},{8,12},{12,16},{16,20},{20,24},{24,28},{28,32},{32,36}... | collective-permute-start | bytes 786440 | tf_op jit(solution)/shard_map/while/body/eval_jaxpr/ppermute | solution.py:13
  177.2 9.8 %collective-permute-start.1 = (f32[128,512]{1,0:T(8,128)S(1)}, f32[128,512]{1,0:T(8,128)S(1)}, u32[]{:S(2)}, u32[]{:S(2)}) collective-permute-start(f32[128,512]{1,0:T(8,128)S(1)} %multiply_add_fusion.8), channel_id=1, source_target_pairs={{0,4},{4,8},{8,12},{12,16},{16,20},{20,24},{24,28},{28,32},{32,36}... | collective-permute-start | bytes 786440 | tf_op jit(solution)/shard_map/while/body/eval_jaxpr/ppermute | solution.py:13
  187.1 9.8 %collective-permute-start.1 = (f32[128,512]{1,0:T(8,128)S(1)}, f32[128,512]{1,0:T(8,128)S(1)}, u32[]{:S(2)}, u32[]{:S(2)}) collective-permute-start(f32[128,512]{1,0:T(8,128)S(1)} %multiply_add_fusion.8), channel_id=1, source_target_pairs={{0,4},{4,8},{8,12},{12,16},{16,20},{20,24},{24,28},{28,32},{32,36}... | collective-permute-start | bytes 786440 | tf_op jit(solution)/shard_map/while/body/eval_jaxpr/ppermute | solution.py:13
  197.0 9.8 %collective-permute-start.1 = (f32[128,512]{1,0:T(8,128)S(1)}, f32[128,512]{1,0:T(8,128)S(1)}, u32[]{:S(2)}, u32[]{:S(2)}) collective-permute-start(f32[128,512]{1,0:T(8,128)S(1)} %multiply_add_fusion.8), channel_id=1, source_target_pairs={{0,4},{4,8},{8,12},{12,16},{16,20},{20,24},{24,28},{28,32},{32,36}... | collective-permute-start | bytes 786440 | tf_op jit(solution)/shard_map/while/body/eval_jaxpr/ppermute | solution.py:13
  206.9 9.8 %collective-permute-start.1 = (f32[128,512]{1,0:T(8,128)S(1)}, f32[128,512]{1,0:T(8,128)S(1)}, u32[]{:S(2)}, u32[]{:S(2)}) collective-permute-start(f32[128,512]{1,0:T(8,128)S(1)} %multiply_add_fusion.8), channel_id=1, source_target_pairs={{0,4},{4,8},{8,12},{12,16},{16,20},{20,24},{24,28},{28,32},{32,36}... | collective-permute-start | bytes 786440 | tf_op jit(solution)/shard_map/while/body/eval_jaxpr/ppermute | solution.py:13
  216.8 9.8 %collective-permute-start.1 = (f32[128,512]{1,0:T(8,128)S(1)}, f32[128,512]{1,0:T(8,128)S(1)}, u32[]{:S(2)}, u32[]{:S(2)}) collective-permute-start(f32[128,512]{1,0:T(8,128)S(1)} %multiply_add_fusion.8), channel_id=1, source_target_pairs={{0,4},{4,8},{8,12},{12,16},{16,20},{20,24},{24,28},{28,32},{32,36}... | collective-permute-start | bytes 786440 | tf_op jit(solution)/shard_map/while/body/eval_jaxpr/ppermute | solution.py:13
  226.7 9.8 %collective-permute-start.1 = (f32[128,512]{1,0:T(8,128)S(1)}, f32[128,512]{1,0:T(8,128)S(1)}, u32[]{:S(2)}, u32[]{:S(2)}) collective-permute-start(f32[128,512]{1,0:T(8,128)S(1)} %multiply_add_fusion.8), channel_id=1, source_target_pairs={{0,4},{4,8},{8,12},{12,16},{16,20},{20,24},{24,28},{28,32},{32,36}... | collective-permute-start | bytes 786440 | tf_op jit(solution)/shard_map/while/body/eval_jaxpr/ppermute | solution.py:13
  236.6 9.8 %collective-permute-start.1 = (f32[128,512]{1,0:T(8,128)S(1)}, f32[128,512]{1,0:T(8,128)S(1)}, u32[]{:S(2)}, u32[]{:S(2)}) collective-permute-start(f32[128,512]{1,0:T(8,128)S(1)} %multiply_add_fusion.8), channel_id=1, source_target_pairs={{0,4},{4,8},{8,12},{12,16},{16,20},{20,24},{24,28},{28,32},{32,36}... | collective-permute-start | bytes 786440 | tf_op jit(solution)/shard_map/while/body/eval_jaxpr/ppermute | solution.py:13
  246.5 9.8 %collective-permute-start.1 = (f32[128,512]{1,0:T(8,128)S(1)}, f32[128,512]{1,0:T(8,128)S(1)}, u32[]{:S(2)}, u32[]{:S(2)}) collective-permute-start(f32[128,512]{1,0:T(8,128)S(1)} %multiply_add_fusion.8), channel_id=1, source_target_pairs={{0,4},{4,8},{8,12},{12,16},{16,20},{20,24},{24,28},{28,32},{32,36}... | collective-permute-start | bytes 786440 | tf_op jit(solution)/shard_map/while/body/eval_jaxpr/ppermute | solution.py:13
  256.4 9.8 %collective-permute-start.1 = (f32[128,512]{1,0:T(8,128)S(1)}, f32[128,512]{1,0:T(8,128)S(1)}, u32[]{:S(2)}, u32[]{:S(2)}) collective-permute-start(f32[128,512]{1,0:T(8,128)S(1)} %multiply_add_fusion.8), channel_id=1, source_target_pairs={{0,4},{4,8},{8,12},{12,16},{16,20},{20,24},{24,28},{28,32},{32,36}... | collective-permute-start | bytes 786440 | tf_op jit(solution)/shard_map/while/body/eval_jaxpr/ppermute | solution.py:13
  266.3 9.8 %collective-permute-start.1 = (f32[128,512]{1,0:T(8,128)S(1)}, f32[128,512]{1,0:T(8,128)S(1)}, u32[]{:S(2)}, u32[]{:S(2)}) collective-permute-start(f32[128,512]{1,0:T(8,128)S(1)} %multiply_add_fusion.8), channel_id=1, source_target_pairs={{0,4},{4,8},{8,12},{12,16},{16,20},{20,24},{24,28},{28,32},{32,36}... | collective-permute-start | bytes 786440 | tf_op jit(solution)/shard_map/while/body/eval_jaxpr/ppermute | solution.py:13
  276.2 9.8 %collective-permute-start.1 = (f32[128,512]{1,0:T(8,128)S(1)}, f32[128,512]{1,0:T(8,128)S(1)}, u32[]{:S(2)}, u32[]{:S(2)}) collective-permute-start(f32[128,512]{1,0:T(8,128)S(1)} %multiply_add_fusion.8), channel_id=1, source_target_pairs={{0,4},{4,8},{8,12},{12,16},{16,20},{20,24},{24,28},{28,32},{32,36}... | collective-permute-start | bytes 786440 | tf_op jit(solution)/shard_map/while/body/eval_jaxpr/ppermute | solution.py:13
  286.1 9.8 %collective-permute-start.1 = (f32[128,512]{1,0:T(8,128)S(1)}, f32[128,512]{1,0:T(8,128)S(1)}, u32[]{:S(2)}, u32[]{:S(2)}) collective-permute-start(f32[128,512]{1,0:T(8,128)S(1)} %multiply_add_fusion.8), channel_id=1, source_target_pairs={{0,4},{4,8},{8,12},{12,16},{16,20},{20,24},{24,28},{28,32},{32,36}... | collective-permute-start | bytes 786440 | tf_op jit(solution)/shard_map/while/body/eval_jaxpr/ppermute | solution.py:13
  296.7 88.0 %reduce-scatter.2.cloned.1.call-start = ((), (), s32[]{:S(2)}) async-start(), calls=%async_computation.1 | async-start | bytes 2621440 | tf_op jit(solution)/shard_map/reduce_scatter | solution.py:60
  300.2 505.8 %all-reduce.6.cloned.1.call-start = ((), (), s32[]{:S(2)}) async-start(), calls=%async_computation.3 | async-start | bytes 4718592 | tf_op jit(solution)/shard_map/psum | solution.py:92
  387.5 7.9 collective-permute-start
  395.5 7.7 collective-permute-start
  403.3 7.7 collective-permute-start
  411.0 7.7 collective-permute-start
  418.8 7.7 collective-permute-start
  426.6 7.7 collective-permute-start
  434.4 7.7 collective-permute-start
  442.2 7.7 collective-permute-start
  450.0 7.7 collective-permute-start
  457.8 7.7 collective-permute-start
  473.3 7.7 collective-permute-start
  481.1 7.7 collective-permute-start
  488.9 9.6 %collective-permute-start = (f32[128,512]{1,0:T(8,128)S(1)}, f32[128,512]{1,0:T(8,128)S(1)}, u32[]{:S(2)}, u32[]{:S(2)}) collective-permute-start(f32[128,512]{1,0:T(8,128)S(1)} %multiply_add_fusion.7), channel_id=1, source_target_pairs={{4,0},{8,4},{12,8},{16,12},{20,16},{24,20},{28,24},{32,28},{36,32}... | collective-permute-start | bytes 786440 | tf_op jit(solution)/shard_map/while/body/eval_jaxpr/ppermute | solution.py:13
  498.6 9.8 %collective-permute-start = (f32[128,512]{1,0:T(8,128)S(1)}, f32[128,512]{1,0:T(8,128)S(1)}, u32[]{:S(2)}, u32[]{:S(2)}) collective-permute-start(f32[128,512]{1,0:T(8,128)S(1)} %multiply_add_fusion.7), channel_id=1, source_target_pairs={{4,0},{8,4},{12,8},{16,12},{20,16},{24,20},{28,24},{32,28},{36,32}... | collective-permute-start | bytes 786440 | tf_op jit(solution)/shard_map/while/body/eval_jaxpr/ppermute | solution.py:13
  508.5 9.8 %collective-permute-start = (f32[128,512]{1,0:T(8,128)S(1)}, f32[128,512]{1,0:T(8,128)S(1)}, u32[]{:S(2)}, u32[]{:S(2)}) collective-permute-start(f32[128,512]{1,0:T(8,128)S(1)} %multiply_add_fusion.7), channel_id=1, source_target_pairs={{4,0},{8,4},{12,8},{16,12},{20,16},{24,20},{28,24},{32,28},{36,32}... | collective-permute-start | bytes 786440 | tf_op jit(solution)/shard_map/while/body/eval_jaxpr/ppermute | solution.py:13
  518.4 9.8 %collective-permute-start = (f32[128,512]{1,0:T(8,128)S(1)}, f32[128,512]{1,0:T(8,128)S(1)}, u32[]{:S(2)}, u32[]{:S(2)}) collective-permute-start(f32[128,512]{1,0:T(8,128)S(1)} %multiply_add_fusion.7), channel_id=1, source_target_pairs={{4,0},{8,4},{12,8},{16,12},{20,16},{24,20},{28,24},{32,28},{36,32}... | collective-permute-start | bytes 786440 | tf_op jit(solution)/shard_map/while/body/eval_jaxpr/ppermute | solution.py:13
  528.3 9.8 %collective-permute-start = (f32[128,512]{1,0:T(8,128)S(1)}, f32[128,512]{1,0:T(8,128)S(1)}, u32[]{:S(2)}, u32[]{:S(2)}) collective-permute-start(f32[128,512]{1,0:T(8,128)S(1)} %multiply_add_fusion.7), channel_id=1, source_target_pairs={{4,0},{8,4},{12,8},{16,12},{20,16},{24,20},{28,24},{32,28},{36,32}... | collective-permute-start | bytes 786440 | tf_op jit(solution)/shard_map/while/body/eval_jaxpr/ppermute | solution.py:13
  538.2 9.8 %collective-permute-start = (f32[128,512]{1,0:T(8,128)S(1)}, f32[128,512]{1,0:T(8,128)S(1)}, u32[]{:S(2)}, u32[]{:S(2)}) collective-permute-start(f32[128,512]{1,0:T(8,128)S(1)} %multiply_add_fusion.7), channel_id=1, source_target_pairs={{4,0},{8,4},{12,8},{16,12},{20,16},{24,20},{28,24},{32,28},{36,32}... | collective-permute-start | bytes 786440 | tf_op jit(solution)/shard_map/while/body/eval_jaxpr/ppermute | solution.py:13
  548.1 9.8 %collective-permute-start = (f32[128,512]{1,0:T(8,128)S(1)}, f32[128,512]{1,0:T(8,128)S(1)}, u32[]{:S(2)}, u32[]{:S(2)}) collective-permute-start(f32[128,512]{1,0:T(8,128)S(1)} %multiply_add_fusion.7), channel_id=1, source_target_pairs={{4,0},{8,4},{12,8},{16,12},{20,16},{24,20},{28,24},{32,28},{36,32}... | collective-permute-start | bytes 786440 | tf_op jit(solution)/shard_map/while/body/eval_jaxpr/ppermute | solution.py:13
  558.0 9.8 %collective-permute-start = (f32[128,512]{1,0:T(8,128)S(1)}, f32[128,512]{1,0:T(8,128)S(1)}, u32[]{:S(2)}, u32[]{:S(2)}) collective-permute-start(f32[128,512]{1,0:T(8,128)S(1)} %multiply_add_fusion.7), channel_id=1, source_target_pairs={{4,0},{8,4},{12,8},{16,12},{20,16},{24,20},{28,24},{32,28},{36,32}... | collective-permute-start | bytes 786440 | tf_op jit(solution)/shard_map/while/body/eval_jaxpr/ppermute | solution.py:13
  567.9 9.8 %collective-permute-start = (f32[128,512]{1,0:T(8,128)S(1)}, f32[128,512]{1,0:T(8,128)S(1)}, u32[]{:S(2)}, u32[]{:S(2)}) collective-permute-start(f32[128,512]{1,0:T(8,128)S(1)} %multiply_add_fusion.7), channel_id=1, source_target_pairs={{4,0},{8,4},{12,8},{16,12},{20,16},{24,20},{28,24},{32,28},{36,32}... | collective-permute-start | bytes 786440 | tf_op jit(solution)/shard_map/while/body/eval_jaxpr/ppermute | solution.py:13
  577.8 9.8 %collective-permute-start = (f32[128,512]{1,0:T(8,128)S(1)}, f32[128,512]{1,0:T(8,128)S(1)}, u32[]{:S(2)}, u32[]{:S(2)}) collective-permute-start(f32[128,512]{1,0:T(8,128)S(1)} %multiply_add_fusion.7), channel_id=1, source_target_pairs={{4,0},{8,4},{12,8},{16,12},{20,16},{24,20},{28,24},{32,28},{36,32}... | collective-permute-start | bytes 786440 | tf_op jit(solution)/shard_map/while/body/eval_jaxpr/ppermute | solution.py:13
  587.7 9.8 %collective-permute-start = (f32[128,512]{1,0:T(8,128)S(1)}, f32[128,512]{1,0:T(8,128)S(1)}, u32[]{:S(2)}, u32[]{:S(2)}) collective-permute-start(f32[128,512]{1,0:T(8,128)S(1)} %multiply_add_fusion.7), channel_id=1, source_target_pairs={{4,0},{8,4},{12,8},{16,12},{20,16},{24,20},{28,24},{32,28},{36,32}... | collective-permute-start | bytes 786440 | tf_op jit(solution)/shard_map/while/body/eval_jaxpr/ppermute | solution.py:13
  597.6 9.8 %collective-permute-start = (f32[128,512]{1,0:T(8,128)S(1)}, f32[128,512]{1,0:T(8,128)S(1)}, u32[]{:S(2)}, u32[]{:S(2)}) collective-permute-start(f32[128,512]{1,0:T(8,128)S(1)} %multiply_add_fusion.7), channel_id=1, source_target_pairs={{4,0},{8,4},{12,8},{16,12},{20,16},{24,20},{28,24},{32,28},{36,32}... | collective-permute-start | bytes 786440 | tf_op jit(solution)/shard_map/while/body/eval_jaxpr/ppermute | solution.py:13
  607.5 9.8 %collective-permute-start = (f32[128,512]{1,0:T(8,128)S(1)}, f32[128,512]{1,0:T(8,128)S(1)}, u32[]{:S(2)}, u32[]{:S(2)}) collective-permute-start(f32[128,512]{1,0:T(8,128)S(1)} %multiply_add_fusion.7), channel_id=1, source_target_pairs={{4,0},{8,4},{12,8},{16,12},{20,16},{24,20},{28,24},{32,28},{36,32}... | collective-permute-start | bytes 786440 | tf_op jit(solution)/shard_map/while/body/eval_jaxpr/ppermute | solution.py:13
  617.4 9.8 %collective-permute-start = (f32[128,512]{1,0:T(8,128)S(1)}, f32[128,512]{1,0:T(8,128)S(1)}, u32[]{:S(2)}, u32[]{:S(2)}) collective-permute-start(f32[128,512]{1,0:T(8,128)S(1)} %multiply_add_fusion.7), channel_id=1, source_target_pairs={{4,0},{8,4},{12,8},{16,12},{20,16},{24,20},{28,24},{32,28},{36,32}... | collective-permute-start | bytes 786440 | tf_op jit(solution)/shard_map/while/body/eval_jaxpr/ppermute | solution.py:13
  627.3 9.8 %collective-permute-start = (f32[128,512]{1,0:T(8,128)S(1)}, f32[128,512]{1,0:T(8,128)S(1)}, u32[]{:S(2)}, u32[]{:S(2)}) collective-permute-start(f32[128,512]{1,0:T(8,128)S(1)} %multiply_add_fusion.7), channel_id=1, source_target_pairs={{4,0},{8,4},{12,8},{16,12},{20,16},{24,20},{28,24},{32,28},{36,32}... | collective-permute-start | bytes 786440 | tf_op jit(solution)/shard_map/while/body/eval_jaxpr/ppermute | solution.py:13
  637.2 9.8 %collective-permute-start = (f32[128,512]{1,0:T(8,128)S(1)}, f32[128,512]{1,0:T(8,128)S(1)}, u32[]{:S(2)}, u32[]{:S(2)}) collective-permute-start(f32[128,512]{1,0:T(8,128)S(1)} %multiply_add_fusion.7), channel_id=1, source_target_pairs={{4,0},{8,4},{12,8},{16,12},{20,16},{24,20},{28,24},{32,28},{36,32}... | collective-permute-start | bytes 786440 | tf_op jit(solution)/shard_map/while/body/eval_jaxpr/ppermute | solution.py:13
  647.1 9.8 %collective-permute-start = (f32[128,512]{1,0:T(8,128)S(1)}, f32[128,512]{1,0:T(8,128)S(1)}, u32[]{:S(2)}, u32[]{:S(2)}) collective-permute-start(f32[128,512]{1,0:T(8,128)S(1)} %multiply_add_fusion.7), channel_id=1, source_target_pairs={{4,0},{8,4},{12,8},{16,12},{20,16},{24,20},{28,24},{32,28},{36,32}... | collective-permute-start | bytes 786440 | tf_op jit(solution)/shard_map/while/body/eval_jaxpr/ppermute | solution.py:13
  657.0 9.8 %collective-permute-start = (f32[128,512]{1,0:T(8,128)S(1)}, f32[128,512]{1,0:T(8,128)S(1)}, u32[]{:S(2)}, u32[]{:S(2)}) collective-permute-start(f32[128,512]{1,0:T(8,128)S(1)} %multiply_add_fusion.7), channel_id=1, source_target_pairs={{4,0},{8,4},{12,8},{16,12},{20,16},{24,20},{28,24},{32,28},{36,32}... | collective-permute-start | bytes 786440 | tf_op jit(solution)/shard_map/while/body/eval_jaxpr/ppermute | solution.py:13
  (9 other events, 602.1 us)
Sparse Core Ops, SparseCore 0:
  296.9 53.3 all-gather.1
  352.6 32.0 reduce-scatter.1
  671.7 134.1 all-reduce.5
where the time goes:
time: 820 us; the launch traced here: 818 us
  waiting for transfers between devices  525 us (64%)
  starting transfers between devices  230 us (28%)
  other arithmetic  24.4 us (3%)
  between operations  14.1 us (2%)
  matrix products  12.6 us (2%)
  local copies, waits for them, and re-layouts  9.91 us (1%)
    ppermute x62, waiting for transfers between devices, passed_along(): lax.ppermute(value, axis, [(source, source + steps) for source in range(f...  318 us
    ppermute x62, starting transfers between devices, passed_along(): lax.ppermute(value, axis, [(source, source + steps) for source in range(f...  230 us
    psum x1, waiting for transfers between devices, body(): grad_b, grad_c = lax.psum((grad_b_part, grad_c_part), 'tm')  134 us
    all_gather x1, waiting for transfers between devices, body(): lax.all_gather(states_bf, 'chan', axis=1, tiled=True)  49.7 us
    reduce_scatter x1, waiting for transfers between devices, body(): lax.psum_scatter(jnp.einsum('kup,fkus->pfs', kernel_c, cot_stack, preferr...  23.6 us
  transfers between devices with their start and end apart: 65, of which 65 were waited for; matrix products, arithmetic and copies ran while one was open for 2% of the time, Pallas kernels for 0%

commit v1 on v0

--- a/solution.py
+++ b/solution.py
@@ -1,3 +1,4 @@
+import functools
 import jax
 import jax.numpy as jnp
 from jax import lax
@@ -5,6 +6,31 @@
 
 W = 64
 offsets = ((-1, -1), (-1, 0), (-1, 1), (0, -1), (0, 0), (0, 1), (1, -1), (1, 0), (1, 1))
+
+
+def _divide_chunk(shard_in, mesh_name):
+    earlier = lax.axis_size(mesh_name)
+    base_arr = lax.axis_index(mesh_name)
+    z2, p_next, piece_out = (earlier, base_arr, shard_in.shape[1])
+    nodes = tuple((dd * z2 if jj == 1 else dd for jj, dd in enumerate(shard_in.shape)))
+    z = jnp.zeros(nodes, shard_in.dtype)
+    extra = x_new = shard_in
+    placed = lax.dynamic_update_slice_in_dim(z, shard_in, p_next * piece_out, axis=1)
+    for j0 in range(1, z2 // 2 + 1):
+        extra = lax.ppermute(extra, mesh_name, tuple(((jj, (jj + 1) % z2) for jj in range(z2))))
+        placed = lax.dynamic_update_slice_in_dim(
+            placed, extra, (p_next - j0) % z2 * piece_out, axis=1
+        )
+        if 2 * j0 < z2:
+            after = tuple(((jj, (jj - 1) % z2) for jj in range(z2)))
+            x_new = lax.ppermute(x_new, mesh_name, after)
+            placed = lax.dynamic_update_slice_in_dim(
+                placed, x_new, (p_next + j0) % z2 * piece_out, axis=1
+            )
+    return placed
+
+
+save_the_spots = functools.partial(_divide_chunk, mesh_name="chan")
 
 
 def passed_along(value, axis, steps):
@@ -85,7 +111,7 @@
     grad_b_part = jnp.einsum(
         "fps,fkcs->kpc", adjoint_bf, input_stack, preferred_element_type=jnp.float32
     )
-    shifted = stencil_stack(lax.all_gather(states_bf, "chan", axis=1, tiled=True), W, 1)
+    shifted = stencil_stack(save_the_spots(states_bf), W, 1)
     grad_c_part = jnp.einsum(
         "fus,fkps->kup", cotangent, shifted, preferred_element_type=jnp.float32
     )

time: 820 us -> 791 us (0.965)
  waiting for transfers between devices: 525 us -> 494 us
    all_gather x1 -> x0, waiting for transfers between devices: 49.7 us -> none  [body(): lax.all_gather(states_bf, 'chan', axis=1, tiled=True)]
    ppermute x62, waiting for transfers between devices: 318 us -> 351 us  [passed_along(): lax.ppermute(value, axis, [(source, source + steps) for source in range(f...]
    reduce_scatter x1, waiting for transfers between devices: 23.6 us -> 0.01 us  [body(): lax.psum_scatter(jnp.einsum('kup,fkus->pfs', kernel_c, cot_stack, preferr...]
    ppermute x0 -> x3, waiting for transfers between devices: none -> 10.4 us  [the longest x2 10.4 us: _divide_chunk(): lax.ppermute(extra, mesh_name, tuple(((jj, (jj + 1) % z2) for jj in range...]
  transfers between devices with their start and end apart: 65 -> 67, of which waited for: 65 -> 65; matrix products, arithmetic and copies ran while one was open for 2% -> 2% of each run, Pallas kernels for 0% -> 0%
where the time goes in v1:
time: 791 us; the launch traced here: 789 us
  waiting for transfers between devices  494 us (62%)
  starting transfers between devices  233 us (29%)
  other arithmetic  23.3 us (3%)
  between operations  14.4 us (2%)
  matrix products  12.6 us (2%)
  local copies, waits for them, and re-layouts  10.1 us (1%)
    ppermute x62, waiting for transfers between devices, passed_along(): lax.ppermute(value, axis, [(source, source + steps) for source in range(f...  351 us
    ppermute x62, starting transfers between devices, passed_along(): lax.ppermute(value, axis, [(source, source + steps) for source in range(f...  229 us
    psum x1, waiting for transfers between devices, body(): grad_b, grad_c = lax.psum((grad_b_part, grad_c_part), 'tm')  132 us
  transfers between devices with their start and end apart: 67, of which 65 were waited for; matrix products, arithmetic and copies ran while one was open for 2% of the time, Pallas kernels for 0%

profile of v1, /device:TPU:1, one launch (start us, length us, event | category | flops | bytes accessed | tf_op | source)
XLA Modules:
  0.0 789.4 jit_solution(17027303213106961504)
XLA Ops:
  25.6 275.2 %while.51 = (s32[]{:T(128)}, f32[128,512]{1,0:T(8,128)S(1)}, f32[128]{0:T(128)S(1)}, f32[128,512]{1,0:T(8,128)S(1)}, s32[]{:T(128)}) while((s32[]{:T(128)}, f32[128,512]{1,0:T(8,128)S(1)}, f32[128]{0:T(128)S(1)}, f32[128,512]{1,0:T(8,128)S(1)}, s32[]{:T(128)}) %tuple.102), condition=%wide.region_12.13_spmd, body=%wide.region_11.12_spmd.sunk | while | flops 131074 | bytes 1835621 | solution.py:80
  25.7 4.9 collective-permute-start.1
  34.1 4.4 collective-permute-start.1
  41.8 4.4 collective-permute-start.1
  49.6 4.4 collective-permute-start.1
  57.4 4.4 collective-permute-start.1
  65.2 4.4 collective-permute-start.1
  73.0 4.4 collective-permute-start.1
  80.8 4.4 collective-permute-start.1
  88.6 4.4 collective-permute-start.1
  104.1 4.4 collective-permute-start.1
  111.9 4.4 collective-permute-start.1
  143.1 6.0 collective-permute-start.1
  152.5 6.5 collective-permute-start.1
  162.4 6.5 collective-permute-start.1
  172.3 6.5 collective-permute-start.1
  182.2 6.5 collective-permute-start.1
  192.1 6.5 collective-permute-start.1
  202.0 6.5 collective-permute-start.1
  211.9 6.5 collective-permute-start.1
  221.8 6.5 collective-permute-start.1
  231.7 6.5 collective-permute-start.1
  241.6 6.5 collective-permute-start.1
  251.5 6.5 collective-permute-start.1
  261.4 6.5 collective-permute-start.1
  271.3 6.5 collective-permute-start.1
  281.2 6.5 collective-permute-start.1
  291.0 6.5 collective-permute-start.1
  304.6 5.3 collective-permute-done.2
  311.2 5.1 collective-permute-done.4
  327.3 312.3 %while.50 = (s32[]{:T(128)}, f32[128,512]{1,0:T(8,128)S(1)}, f32[128]{0:T(128)S(1)}, f32[128,512]{1,0:T(8,128)S(1)}, s32[]{:T(128)}) while((s32[]{:T(128)}, f32[128,512]{1,0:T(8,128)S(1)}, f32[128]{0:T(128)S(1)}, f32[128,512]{1,0:T(8,128)S(1)}, s32[]{:T(128)}) %tuple.112), condition=%wide.region_6.7_spmd, body=%wide.region_5.6_spmd.sunk | while | flops 131074 | bytes 1835621 | solution.py:105
  329.3 10.6 %collective-permute-done = f32[128,512]{1,0:T(8,128)S(1)} collective-permute-done((f32[128,512]{1,0:T(8,128)S(1)}, f32[128,512]{1,0:T(8,128)S(1)}, u32[]{:S(2)}, u32[]{:S(2)}) %collective-permute-start) | collective-permute-done | bytes 262176 | tf_op jit(solution)/shard_map/while/body/eval_jaxpr/ppermute | solution.py:39
  341.9 5.8 collective-permute-done
  349.7 10.6 %collective-permute-done = f32[128,512]{1,0:T(8,128)S(1)} collective-permute-done((f32[128,512]{1,0:T(8,128)S(1)}, f32[128,512]{1,0:T(8,128)S(1)}, u32[]{:S(2)}, u32[]{:S(2)}) %collective-permute-start) | collective-permute-done | bytes 262176 | tf_op jit(solution)/shard_map/while/body/eval_jaxpr/ppermute | solution.py:39
  362.3 5.8 collective-permute-done
  370.1 10.6 %collective-permute-done = f32[128,512]{1,0:T(8,128)S(1)} collective-permute-done((f32[128,512]{1,0:T(8,128)S(1)}, f32[128,512]{1,0:T(8,128)S(1)}, u32[]{:S(2)}, u32[]{:S(2)}) %collective-permute-start) | collective-permute-done | bytes 262176 | tf_op jit(solution)/shard_map/while/body/eval_jaxpr/ppermute | solution.py:39
  382.7 5.8 collective-permute-done
  390.5 11.5 %collective-permute-done = f32[128,512]{1,0:T(8,128)S(1)} collective-permute-done((f32[128,512]{1,0:T(8,128)S(1)}, f32[128,512]{1,0:T(8,128)S(1)}, u32[]{:S(2)}, u32[]{:S(2)}) %collective-permute-start) | collective-permute-done | bytes 262176 | tf_op jit(solution)/shard_map/while/body/eval_jaxpr/ppermute | solution.py:39
  404.0 7.9 collective-permute-done
  413.9 7.9 collective-permute-done
  423.8 7.9 collective-permute-done
  433.7 7.9 collective-permute-done
  443.6 7.9 collective-permute-done
  453.5 7.9 collective-permute-done
  463.4 7.9 collective-permute-done
  473.3 7.9 collective-permute-done
  483.2 7.9 collective-permute-done
  493.1 7.9 collective-permute-done
  503.0 7.9 collective-permute-done
  512.9 7.9 collective-permute-done
  522.8 7.9 collective-permute-done
  532.7 7.9 collective-permute-done
  542.6 7.9 collective-permute-done
  552.5 7.9 collective-permute-done
  562.4 7.9 collective-permute-done
  572.3 7.9 collective-permute-done
  582.2 7.9 collective-permute-done
  592.1 7.9 collective-permute-done
  602.0 7.9 collective-permute-done
  611.8 7.9 collective-permute-done
  621.7 7.9 collective-permute-done
  631.6 7.9 collective-permute-done
  639.5 4.8 convolution_bitcast_fusion.2
  645.2 132.3 %all-reduce.6.cloned.1.call-done = (f32[9,128,256]{1,2,0:T(8,128)}, f32[9,64,512]{2,1,0:T(8,128)}) async-done(((f32[9,128,256]{1,2,0:T(8,128)}, f32[9,64,512]{2,1,0:T(8,128)}), (f32[9,128,256]{1,2,0:T(8,128)}, f32[9,64,512]{2,1,0:T(8,128)})) %all-reduce.6.cloned.1.call-update) | async-done | bytes 2359312 | tf_op jit(solution)/shard_map/psum | solution.py:118
  (224 shorter events, 227.5 us)
Async XLA Ops:
  7.2 317.4 %reduce-scatter.2.cloned.1.call-start = ((), (), s32[]{:S(2)}) async-start(), calls=%async_computation.1 | async-start | bytes 2621440 | tf_op jit(solution)/shard_map/reduce_scatter | solution.py:86
  18.8 758.7 %all-reduce.6.cloned.1.call-start = ((), (), s32[]{:S(2)}) async-start(), calls=%async_computation.2 | async-start | bytes 4718592 | tf_op jit(solution)/shard_map/psum | solution.py:118
  25.7 8.2 %collective-permute-start.1 = (f32[128,512]{1,0:T(8,128)S(1)}, f32[128,512]{1,0:T(8,128)S(1)}, u32[]{:S(2)}, u32[]{:S(2)}) collective-permute-start(f32[128,512]{1,0:T(8,128)S(1)} %multiply_add_fusion.8), channel_id=1, source_target_pairs={{0,4},{4,8},{8,12},{12,16},{16,20},{20,24},{24,28},{28,32},{32,36}... | collective-permute-start | bytes 786440 | tf_op jit(solution)/shard_map/while/body/eval_jaxpr/ppermute | solution.py:39
  34.1 7.7 collective-permute-start.1
  41.8 7.7 collective-permute-start.1
  49.6 7.7 collective-permute-start.1
  57.4 7.7 collective-permute-start.1
  65.2 7.7 collective-permute-start.1
  73.0 7.7 collective-permute-start.1
  80.8 7.7 collective-permute-start.1
  88.6 7.7 collective-permute-start.1
  96.4 7.7 collective-permute-start.1
  104.1 7.7 collective-permute-start.1
  111.9 7.7 collective-permute-start.1
  119.7 7.7 collective-permute-start.1
  143.1 9.3 %collective-permute-start.1 = (f32[128,512]{1,0:T(8,128)S(1)}, f32[128,512]{1,0:T(8,128)S(1)}, u32[]{:S(2)}, u32[]{:S(2)}) collective-permute-start(f32[128,512]{1,0:T(8,128)S(1)} %multiply_add_fusion.8), channel_id=1, source_target_pairs={{0,4},{4,8},{8,12},{12,16},{16,20},{20,24},{24,28},{28,32},{32,36}... | collective-permute-start | bytes 786440 | tf_op jit(solution)/shard_map/while/body/eval_jaxpr/ppermute | solution.py:39
  152.5 9.8 %collective-permute-start.1 = (f32[128,512]{1,0:T(8,128)S(1)}, f32[128,512]{1,0:T(8,128)S(1)}, u32[]{:S(2)}, u32[]{:S(2)}) collective-permute-start(f32[128,512]{1,0:T(8,128)S(1)} %multiply_add_fusion.8), channel_id=1, source_target_pairs={{0,4},{4,8},{8,12},{12,16},{16,20},{20,24},{24,28},{28,32},{32,36}... | collective-permute-start | bytes 786440 | tf_op jit(solution)/shard_map/while/body/eval_jaxpr/ppermute | solution.py:39
  162.4 9.8 %collective-permute-start.1 = (f32[128,512]{1,0:T(8,128)S(1)}, f32[128,512]{1,0:T(8,128)S(1)}, u32[]{:S(2)}, u32[]{:S(2)}) collective-permute-start(f32[128,512]{1,0:T(8,128)S(1)} %multiply_add_fusion.8), channel_id=1, source_target_pairs={{0,4},{4,8},{8,12},{12,16},{16,20},{20,24},{24,28},{28,32},{32,36}... | collective-permute-start | bytes 786440 | tf_op jit(solution)/shard_map/while/body/eval_jaxpr/ppermute | solution.py:39
  172.3 9.8 %collective-permute-start.1 = (f32[128,512]{1,0:T(8,128)S(1)}, f32[128,512]{1,0:T(8,128)S(1)}, u32[]{:S(2)}, u32[]{:S(2)}) collective-permute-start(f32[128,512]{1,0:T(8,128)S(1)} %multiply_add_fusion.8), channel_id=1, source_target_pairs={{0,4},{4,8},{8,12},{12,16},{16,20},{20,24},{24,28},{28,32},{32,36}... | collective-permute-start | bytes 786440 | tf_op jit(solution)/shard_map/while/body/eval_jaxpr/ppermute | solution.py:39
  182.2 9.8 %collective-permute-start.1 = (f32[128,512]{1,0:T(8,128)S(1)}, f32[128,512]{1,0:T(8,128)S(1)}, u32[]{:S(2)}, u32[]{:S(2)}) collective-permute-start(f32[128,512]{1,0:T(8,128)S(1)} %multiply_add_fusion.8), channel_id=1, source_target_pairs={{0,4},{4,8},{8,12},{12,16},{16,20},{20,24},{24,28},{28,32},{32,36}... | collective-permute-start | bytes 786440 | tf_op jit(solution)/shard_map/while/body/eval_jaxpr/ppermute | solution.py:39
  192.1 9.8 %collective-permute-start.1 = (f32[128,512]{1,0:T(8,128)S(1)}, f32[128,512]{1,0:T(8,128)S(1)}, u32[]{:S(2)}, u32[]{:S(2)}) collective-permute-start(f32[128,512]{1,0:T(8,128)S(1)} %multiply_add_fusion.8), channel_id=1, source_target_pairs={{0,4},{4,8},{8,12},{12,16},{16,20},{20,24},{24,28},{28,32},{32,36}... | collective-permute-start | bytes 786440 | tf_op jit(solution)/shard_map/while/body/eval_jaxpr/ppermute | solution.py:39
  202.0 9.8 %collective-permute-start.1 = (f32[128,512]{1,0:T(8,128)S(1)}, f32[128,512]{1,0:T(8,128)S(1)}, u32[]{:S(2)}, u32[]{:S(2)}) collective-permute-start(f32[128,512]{1,0:T(8,128)S(1)} %multiply_add_fusion.8), channel_id=1, source_target_pairs={{0,4},{4,8},{8,12},{12,16},{16,20},{20,24},{24,28},{28,32},{32,36}... | collective-permute-start | bytes 786440 | tf_op jit(solution)/shard_map/while/body/eval_jaxpr/ppermute | solution.py:39
  211.9 9.8 %collective-permute-start.1 = (f32[128,512]{1,0:T(8,128)S(1)}, f32[128,512]{1,0:T(8,128)S(1)}, u32[]{:S(2)}, u32[]{:S(2)}) collective-permute-start(f32[128,512]{1,0:T(8,128)S(1)} %multiply_add_fusion.8), channel_id=1, source_target_pairs={{0,4},{4,8},{8,12},{12,16},{16,20},{20,24},{24,28},{28,32},{32,36}... | collective-permute-start | bytes 786440 | tf_op jit(solution)/shard_map/while/body/eval_jaxpr/ppermute | solution.py:39
  221.8 9.8 %collective-permute-start.1 = (f32[128,512]{1,0:T(8,128)S(1)}, f32[128,512]{1,0:T(8,128)S(1)}, u32[]{:S(2)}, u32[]{:S(2)}) collective-permute-start(f32[128,512]{1,0:T(8,128)S(1)} %multiply_add_fusion.8), channel_id=1, source_target_pairs={{0,4},{4,8},{8,12},{12,16},{16,20},{20,24},{24,28},{28,32},{32,36}... | collective-permute-start | bytes 786440 | tf_op jit(solution)/shard_map/while/body/eval_jaxpr/ppermute | solution.py:39
  231.7 9.8 %collective-permute-start.1 = (f32[128,512]{1,0:T(8,128)S(1)}, f32[128,512]{1,0:T(8,128)S(1)}, u32[]{:S(2)}, u32[]{:S(2)}) collective-permute-start(f32[128,512]{1,0:T(8,128)S(1)} %multiply_add_fusion.8), channel_id=1, source_target_pairs={{0,4},{4,8},{8,12},{12,16},{16,20},{20,24},{24,28},{28,32},{32,36}... | collective-permute-start | bytes 786440 | tf_op jit(solution)/shard_map/while/body/eval_jaxpr/ppermute | solution.py:39
  241.6 9.8 %collective-permute-start.1 = (f32[128,512]{1,0:T(8,128)S(1)}, f32[128,512]{1,0:T(8,128)S(1)}, u32[]{:S(2)}, u32[]{:S(2)}) collective-permute-start(f32[128,512]{1,0:T(8,128)S(1)} %multiply_add_fusion.8), channel_id=1, source_target_pairs={{0,4},{4,8},{8,12},{12,16},{16,20},{20,24},{24,28},{28,32},{32,36}... | collective-permute-start | bytes 786440 | tf_op jit(solution)/shard_map/while/body/eval_jaxpr/ppermute | solution.py:39
  251.5 9.8 %collective-permute-start.1 = (f32[128,512]{1,0:T(8,128)S(1)}, f32[128,512]{1,0:T(8,128)S(1)}, u32[]{:S(2)}, u32[]{:S(2)}) collective-permute-start(f32[128,512]{1,0:T(8,128)S(1)} %multiply_add_fusion.8), channel_id=1, source_target_pairs={{0,4},{4,8},{8,12},{12,16},{16,20},{20,24},{24,28},{28,32},{32,36}... | collective-permute-start | bytes 786440 | tf_op jit(solution)/shard_map/while/body/eval_jaxpr/ppermute | solution.py:39
  261.4 9.8 %collective-permute-start.1 = (f32[128,512]{1,0:T(8,128)S(1)}, f32[128,512]{1,0:T(8,128)S(1)}, u32[]{:S(2)}, u32[]{:S(2)}) collective-permute-start(f32[128,512]{1,0:T(8,128)S(1)} %multiply_add_fusion.8), channel_id=1, source_target_pairs={{0,4},{4,8},{8,12},{12,16},{16,20},{20,24},{24,28},{28,32},{32,36}... | collective-permute-start | bytes 786440 | tf_op jit(solution)/shard_map/while/body/eval_jaxpr/ppermute | solution.py:39
  271.3 9.8 %collective-permute-start.1 = (f32[128,512]{1,0:T(8,128)S(1)}, f32[128,512]{1,0:T(8,128)S(1)}, u32[]{:S(2)}, u32[]{:S(2)}) collective-permute-start(f32[128,512]{1,0:T(8,128)S(1)} %multiply_add_fusion.8), channel_id=1, source_target_pairs={{0,4},{4,8},{8,12},{12,16},{16,20},{20,24},{24,28},{28,32},{32,36}... | collective-permute-start | bytes 786440 | tf_op jit(solution)/shard_map/while/body/eval_jaxpr/ppermute | solution.py:39
  281.2 9.8 %collective-permute-start.1 = (f32[128,512]{1,0:T(8,128)S(1)}, f32[128,512]{1,0:T(8,128)S(1)}, u32[]{:S(2)}, u32[]{:S(2)}) collective-permute-start(f32[128,512]{1,0:T(8,128)S(1)} %multiply_add_fusion.8), channel_id=1, source_target_pairs={{0,4},{4,8},{8,12},{12,16},{16,20},{20,24},{24,28},{28,32},{32,36}... | collective-permute-start | bytes 786440 | tf_op jit(solution)/shard_map/while/body/eval_jaxpr/ppermute | solution.py:39
  291.0 9.8 %collective-permute-start.1 = (f32[128,512]{1,0:T(8,128)S(1)}, f32[128,512]{1,0:T(8,128)S(1)}, u32[]{:S(2)}, u32[]{:S(2)}) collective-permute-start(f32[128,512]{1,0:T(8,128)S(1)} %multiply_add_fusion.8), channel_id=1, source_target_pairs={{0,4},{4,8},{8,12},{12,16},{16,20},{20,24},{24,28},{28,32},{32,36}... | collective-permute-start | bytes 786440 | tf_op jit(solution)/shard_map/while/body/eval_jaxpr/ppermute | solution.py:39
  301.8 8.1 %collective-permute-start.2 = (bf16[2,128,512]{2,1,0:T(8,128)(2,1)}, bf16[2,128,512]{2,1,0:T(8,128)(2,1)S(1)}, u32[]{:S(2)}, u32[]{:S(2)}) collective-permute-start(bf16[2,128,512]{2,1,0:T(8,128)(2,1)} %get-tuple-element.275), channel_id=1, source_target_pairs={{0,1},{1,2},{2,3},{3,0},{4,5},{5,6},{6,7},{7,4},{8,9},{9,10},{10,1... | collective-permute-start | bytes 786440 | tf_op jit(solution)/shard_map/ppermute | solution.py:20
  303.1 8.0 %collective-permute-start.3 = (bf16[2,128,512]{2,1,0:T(8,128)(2,1)}, bf16[2,128,512]{2,1,0:T(8,128)(2,1)S(1)}, u32[]{:S(2)}, u32[]{:S(2)}) collective-permute-start(bf16[2,128,512]{2,1,0:T(8,128)(2,1)} %get-tuple-element.275), channel_id=1, source_target_pairs={{0,3},{1,0},{2,1},{3,2},{4,7},{5,4},{6,5},{7,6},{8,11},{9,8},{10,9... | collective-permute-start | bytes 786440 | tf_op jit(solution)/shard_map/ppermute | solution.py:26
  327.4 12.5 %collective-permute-start = (f32[128,512]{1,0:T(8,128)S(1)}, f32[128,512]{1,0:T(8,128)S(1)}, u32[]{:S(2)}, u32[]{:S(2)}) collective-permute-start(f32[128,512]{1,0:T(8,128)S(1)} %multiply_add_fusion.7), channel_id=1, source_target_pairs={{4,0},{8,4},{12,8},{16,12},{20,16},{24,20},{28,24},{32,28},{36,32}... | collective-permute-start | bytes 786440 | tf_op jit(solution)/shard_map/while/body/eval_jaxpr/ppermute | solution.py:39
  340.0 7.7 collective-permute-start
  347.8 12.5 %collective-permute-start = (f32[128,512]{1,0:T(8,128)S(1)}, f32[128,512]{1,0:T(8,128)S(1)}, u32[]{:S(2)}, u32[]{:S(2)}) collective-permute-start(f32[128,512]{1,0:T(8,128)S(1)} %multiply_add_fusion.7), channel_id=1, source_target_pairs={{4,0},{8,4},{12,8},{16,12},{20,16},{24,20},{28,24},{32,28},{36,32}... | collective-permute-start | bytes 786440 | tf_op jit(solution)/shard_map/while/body/eval_jaxpr/ppermute | solution.py:39
  360.4 7.7 collective-permute-start
  368.2 12.5 %collective-permute-start = (f32[128,512]{1,0:T(8,128)S(1)}, f32[128,512]{1,0:T(8,128)S(1)}, u32[]{:S(2)}, u32[]{:S(2)}) collective-permute-start(f32[128,512]{1,0:T(8,128)S(1)} %multiply_add_fusion.7), channel_id=1, source_target_pairs={{4,0},{8,4},{12,8},{16,12},{20,16},{24,20},{28,24},{32,28},{36,32}... | collective-permute-start | bytes 786440 | tf_op jit(solution)/shard_map/while/body/eval_jaxpr/ppermute | solution.py:39
  380.8 7.7 collective-permute-start
  388.6 13.4 %collective-permute-start = (f32[128,512]{1,0:T(8,128)S(1)}, f32[128,512]{1,0:T(8,128)S(1)}, u32[]{:S(2)}, u32[]{:S(2)}) collective-permute-start(f32[128,512]{1,0:T(8,128)S(1)} %multiply_add_fusion.7), channel_id=1, source_target_pairs={{4,0},{8,4},{12,8},{16,12},{20,16},{24,20},{28,24},{32,28},{36,32}... | collective-permute-start | bytes 786440 | tf_op jit(solution)/shard_map/while/body/eval_jaxpr/ppermute | solution.py:39
  402.1 9.8 %collective-permute-start = (f32[128,512]{1,0:T(8,128)S(1)}, f32[128,512]{1,0:T(8,128)S(1)}, u32[]{:S(2)}, u32[]{:S(2)}) collective-permute-start(f32[128,512]{1,0:T(8,128)S(1)} %multiply_add_fusion.7), channel_id=1, source_target_pairs={{4,0},{8,4},{12,8},{16,12},{20,16},{24,20},{28,24},{32,28},{36,32}... | collective-permute-start | bytes 786440 | tf_op jit(solution)/shard_map/while/body/eval_jaxpr/ppermute | solution.py:39
  412.0 9.8 %collective-permute-start = (f32[128,512]{1,0:T(8,128)S(1)}, f32[128,512]{1,0:T(8,128)S(1)}, u32[]{:S(2)}, u32[]{:S(2)}) collective-permute-start(f32[128,512]{1,0:T(8,128)S(1)} %multiply_add_fusion.7), channel_id=1, source_target_pairs={{4,0},{8,4},{12,8},{16,12},{20,16},{24,20},{28,24},{32,28},{36,32}... | collective-permute-start | bytes 786440 | tf_op jit(solution)/shard_map/while/body/eval_jaxpr/ppermute | solution.py:39
  421.9 9.8 %collective-permute-start = (f32[128,512]{1,0:T(8,128)S(1)}, f32[128,512]{1,0:T(8,128)S(1)}, u32[]{:S(2)}, u32[]{:S(2)}) collective-permute-start(f32[128,512]{1,0:T(8,128)S(1)} %multiply_add_fusion.7), channel_id=1, source_target_pairs={{4,0},{8,4},{12,8},{16,12},{20,16},{24,20},{28,24},{32,28},{36,32}... | collective-permute-start | bytes 786440 | tf_op jit(solution)/shard_map/while/body/eval_jaxpr/ppermute | solution.py:39
  431.8 9.8 %collective-permute-start = (f32[128,512]{1,0:T(8,128)S(1)}, f32[128,512]{1,0:T(8,128)S(1)}, u32[]{:S(2)}, u32[]{:S(2)}) collective-permute-start(f32[128,512]{1,0:T(8,128)S(1)} %multiply_add_fusion.7), channel_id=1, source_target_pairs={{4,0},{8,4},{12,8},{16,12},{20,16},{24,20},{28,24},{32,28},{36,32}... | collective-permute-start | bytes 786440 | tf_op jit(solution)/shard_map/while/body/eval_jaxpr/ppermute | solution.py:39
  441.7 9.8 %collective-permute-start = (f32[128,512]{1,0:T(8,128)S(1)}, f32[128,512]{1,0:T(8,128)S(1)}, u32[]{:S(2)}, u32[]{:S(2)}) collective-permute-start(f32[128,512]{1,0:T(8,128)S(1)} %multiply_add_fusion.7), channel_id=1, source_target_pairs={{4,0},{8,4},{12,8},{16,12},{20,16},{24,20},{28,24},{32,28},{36,32}... | collective-permute-start | bytes 786440 | tf_op jit(solution)/shard_map/while/body/eval_jaxpr/ppermute | solution.py:39
  451.6 9.8 %collective-permute-start = (f32[128,512]{1,0:T(8,128)S(1)}, f32[128,512]{1,0:T(8,128)S(1)}, u32[]{:S(2)}, u32[]{:S(2)}) collective-permute-start(f32[128,512]{1,0:T(8,128)S(1)} %multiply_add_fusion.7), channel_id=1, source_target_pairs={{4,0},{8,4},{12,8},{16,12},{20,16},{24,20},{28,24},{32,28},{36,32}... | collective-permute-start | bytes 786440 | tf_op jit(solution)/shard_map/while/body/eval_jaxpr/ppermute | solution.py:39
  461.5 9.8 %collective-permute-start = (f32[128,512]{1,0:T(8,128)S(1)}, f32[128,512]{1,0:T(8,128)S(1)}, u32[]{:S(2)}, u32[]{:S(2)}) collective-permute-start(f32[128,512]{1,0:T(8,128)S(1)} %multiply_add_fusion.7), channel_id=1, source_target_pairs={{4,0},{8,4},{12,8},{16,12},{20,16},{24,20},{28,24},{32,28},{36,32}... | collective-permute-start | bytes 786440 | tf_op jit(solution)/shard_map/while/body/eval_jaxpr/ppermute | solution.py:39
  471.4 9.8 %collective-permute-start = (f32[128,512]{1,0:T(8,128)S(1)}, f32[128,512]{1,0:T(8,128)S(1)}, u32[]{:S(2)}, u32[]{:S(2)}) collective-permute-start(f32[128,512]{1,0:T(8,128)S(1)} %multiply_add_fusion.7), channel_id=1, source_target_pairs={{4,0},{8,4},{12,8},{16,12},{20,16},{24,20},{28,24},{32,28},{36,32}... | collective-permute-start | bytes 786440 | tf_op jit(solution)/shard_map/while/body/eval_jaxpr/ppermute | solution.py:39
  481.3 9.8 %collective-permute-start = (f32[128,512]{1,0:T(8,128)S(1)}, f32[128,512]{1,0:T(8,128)S(1)}, u32[]{:S(2)}, u32[]{:S(2)}) collective-permute-start(f32[128,512]{1,0:T(8,128)S(1)} %multiply_add_fusion.7), channel_id=1, source_target_pairs={{4,0},{8,4},{12,8},{16,12},{20,16},{24,20},{28,24},{32,28},{36,32}... | collective-permute-start | bytes 786440 | tf_op jit(solution)/shard_map/while/body/eval_jaxpr/ppermute | solution.py:39
  491.2 9.8 %collective-permute-start = (f32[128,512]{1,0:T(8,128)S(1)}, f32[128,512]{1,0:T(8,128)S(1)}, u32[]{:S(2)}, u32[]{:S(2)}) collective-permute-start(f32[128,512]{1,0:T(8,128)S(1)} %multiply_add_fusion.7), channel_id=1, source_target_pairs={{4,0},{8,4},{12,8},{16,12},{20,16},{24,20},{28,24},{32,28},{36,32}... | collective-permute-start | bytes 786440 | tf_op jit(solution)/shard_map/while/body/eval_jaxpr/ppermute | solution.py:39
  501.1 9.8 %collective-permute-start = (f32[128,512]{1,0:T(8,128)S(1)}, f32[128,512]{1,0:T(8,128)S(1)}, u32[]{:S(2)}, u32[]{:S(2)}) collective-permute-start(f32[128,512]{1,0:T(8,128)S(1)} %multiply_add_fusion.7), channel_id=1, source_target_pairs={{4,0},{8,4},{12,8},{16,12},{20,16},{24,20},{28,24},{32,28},{36,32}... | collective-permute-start | bytes 786440 | tf_op jit(solution)/shard_map/while/body/eval_jaxpr/ppermute | solution.py:39
  511.0 9.8 %collective-permute-start = (f32[128,512]{1,0:T(8,128)S(1)}, f32[128,512]{1,0:T(8,128)S(1)}, u32[]{:S(2)}, u32[]{:S(2)}) collective-permute-start(f32[128,512]{1,0:T(8,128)S(1)} %multiply_add_fusion.7), channel_id=1, source_target_pairs={{4,0},{8,4},{12,8},{16,12},{20,16},{24,20},{28,24},{32,28},{36,32}... | collective-permute-start | bytes 786440 | tf_op jit(solution)/shard_map/while/body/eval_jaxpr/ppermute | solution.py:39
  520.9 9.8 %collective-permute-start = (f32[128,512]{1,0:T(8,128)S(1)}, f32[128,512]{1,0:T(8,128)S(1)}, u32[]{:S(2)}, u32[]{:S(2)}) collective-permute-start(f32[128,512]{1,0:T(8,128)S(1)} %multiply_add_fusion.7), channel_id=1, source_target_pairs={{4,0},{8,4},{12,8},{16,12},{20,16},{24,20},{28,24},{32,28},{36,32}... | collective-permute-start | bytes 786440 | tf_op jit(solution)/shard_map/while/body/eval_jaxpr/ppermute | solution.py:39
  530.8 9.8 %collective-permute-start = (f32[128,512]{1,0:T(8,128)S(1)}, f32[128,512]{1,0:T(8,128)S(1)}, u32[]{:S(2)}, u32[]{:S(2)}) collective-permute-start(f32[128,512]{1,0:T(8,128)S(1)} %multiply_add_fusion.7), channel_id=1, source_target_pairs={{4,0},{8,4},{12,8},{16,12},{20,16},{24,20},{28,24},{32,28},{36,32}... | collective-permute-start | bytes 786440 | tf_op jit(solution)/shard_map/while/body/eval_jaxpr/ppermute | solution.py:39
  540.6 9.8 %collective-permute-start = (f32[128,512]{1,0:T(8,128)S(1)}, f32[128,512]{1,0:T(8,128)S(1)}, u32[]{:S(2)}, u32[]{:S(2)}) collective-permute-start(f32[128,512]{1,0:T(8,128)S(1)} %multiply_add_fusion.7), channel_id=1, source_target_pairs={{4,0},{8,4},{12,8},{16,12},{20,16},{24,20},{28,24},{32,28},{36,32}... | collective-permute-start | bytes 786440 | tf_op jit(solution)/shard_map/while/body/eval_jaxpr/ppermute | solution.py:39
  550.5 9.8 %collective-permute-start = (f32[128,512]{1,0:T(8,128)S(1)}, f32[128,512]{1,0:T(8,128)S(1)}, u32[]{:S(2)}, u32[]{:S(2)}) collective-permute-start(f32[128,512]{1,0:T(8,128)S(1)} %multiply_add_fusion.7), channel_id=1, source_target_pairs={{4,0},{8,4},{12,8},{16,12},{20,16},{24,20},{28,24},{32,28},{36,32}... | collective-permute-start | bytes 786440 | tf_op jit(solution)/shard_map/while/body/eval_jaxpr/ppermute | solution.py:39
  560.4 9.8 %collective-permute-start = (f32[128,512]{1,0:T(8,128)S(1)}, f32[128,512]{1,0:T(8,128)S(1)}, u32[]{:S(2)}, u32[]{:S(2)}) collective-permute-start(f32[128,512]{1,0:T(8,128)S(1)} %multiply_add_fusion.7), channel_id=1, source_target_pairs={{4,0},{8,4},{12,8},{16,12},{20,16},{24,20},{28,24},{32,28},{36,32}... | collective-permute-start | bytes 786440 | tf_op jit(solution)/shard_map/while/body/eval_jaxpr/ppermute | solution.py:39
  570.3 9.8 %collective-permute-start = (f32[128,512]{1,0:T(8,128)S(1)}, f32[128,512]{1,0:T(8,128)S(1)}, u32[]{:S(2)}, u32[]{:S(2)}) collective-permute-start(f32[128,512]{1,0:T(8,128)S(1)} %multiply_add_fusion.7), channel_id=1, source_target_pairs={{4,0},{8,4},{12,8},{16,12},{20,16},{24,20},{28,24},{32,28},{36,32}... | collective-permute-start | bytes 786440 | tf_op jit(solution)/shard_map/while/body/eval_jaxpr/ppermute | solution.py:39
  580.2 9.8 %collective-permute-start = (f32[128,512]{1,0:T(8,128)S(1)}, f32[128,512]{1,0:T(8,128)S(1)}, u32[]{:S(2)}, u32[]{:S(2)}) collective-permute-start(f32[128,512]{1,0:T(8,128)S(1)} %multiply_add_fusion.7), channel_id=1, source_target_pairs={{4,0},{8,4},{12,8},{16,12},{20,16},{24,20},{28,24},{32,28},{36,32}... | collective-permute-start | bytes 786440 | tf_op jit(solution)/shard_map/while/body/eval_jaxpr/ppermute | solution.py:39
  590.1 9.8 %collective-permute-start = (f32[128,512]{1,0:T(8,128)S(1)}, f32[128,512]{1,0:T(8,128)S(1)}, u32[]{:S(2)}, u32[]{:S(2)}) collective-permute-start(f32[128,512]{1,0:T(8,128)S(1)} %multiply_add_fusion.7), channel_id=1, source_target_pairs={{4,0},{8,4},{12,8},{16,12},{20,16},{24,20},{28,24},{32,28},{36,32}... | collective-permute-start | bytes 786440 | tf_op jit(solution)/shard_map/while/body/eval_jaxpr/ppermute | solution.py:39
  600.0 9.8 %collective-permute-start = (f32[128,512]{1,0:T(8,128)S(1)}, f32[128,512]{1,0:T(8,128)S(1)}, u32[]{:S(2)}, u32[]{:S(2)}) collective-permute-start(f32[128,512]{1,0:T(8,128)S(1)} %multiply_add_fusion.7), channel_id=1, source_target_pairs={{4,0},{8,4},{12,8},{16,12},{20,16},{24,20},{28,24},{32,28},{36,32}... | collective-permute-start | bytes 786440 | tf_op jit(solution)/shard_map/while/body/eval_jaxpr/ppermute | solution.py:39
  609.9 9.8 %collective-permute-start = (f32[128,512]{1,0:T(8,128)S(1)}, f32[128,512]{1,0:T(8,128)S(1)}, u32[]{:S(2)}, u32[]{:S(2)}) collective-permute-start(f32[128,512]{1,0:T(8,128)S(1)} %multiply_add_fusion.7), channel_id=1, source_target_pairs={{4,0},{8,4},{12,8},{16,12},{20,16},{24,20},{28,24},{32,28},{36,32}... | collective-permute-start | bytes 786440 | tf_op jit(solution)/shard_map/while/body/eval_jaxpr/ppermute | solution.py:39
  619.8 9.8 %collective-permute-start = (f32[128,512]{1,0:T(8,128)S(1)}, f32[128,512]{1,0:T(8,128)S(1)}, u32[]{:S(2)}, u32[]{:S(2)}) collective-permute-start(f32[128,512]{1,0:T(8,128)S(1)} %multiply_add_fusion.7), channel_id=1, source_target_pairs={{4,0},{8,4},{12,8},{16,12},{20,16},{24,20},{28,24},{32,28},{36,32}... | collective-permute-start | bytes 786440 | tf_op jit(solution)/shard_map/while/body/eval_jaxpr/ppermute | solution.py:39
  629.7 9.8 %collective-permute-start = (f32[128,512]{1,0:T(8,128)S(1)}, f32[128,512]{1,0:T(8,128)S(1)}, u32[]{:S(2)}, u32[]{:S(2)}) collective-permute-start(f32[128,512]{1,0:T(8,128)S(1)} %multiply_add_fusion.7), channel_id=1, source_target_pairs={{4,0},{8,4},{12,8},{16,12},{20,16},{24,20},{28,24},{32,28},{36,32}... | collective-permute-start | bytes 786440 | tf_op jit(solution)/shard_map/while/body/eval_jaxpr/ppermute | solution.py:39
  (10 other events, 330.3 us)
Sparse Core Ops, SparseCore 0:
  19.0 32.8 reduce-scatter.1
  644.5 132.9 all-reduce.5
